TPU v7x, 512 devices: a whole 4x8x8 slice. The times are simulated.
512 devices in a mesh: dp: 128 (over z, y, core), proto: 4 (over x).
Axes of the slice: x: 4, y: 8, z: 8, core: 2. Of those that a mesh axis runs over, the one named last changes fastest.
Arguments:
- teacher_emb: bfloat16 [32768, 128], P('dp'), may hold values from -64 to 64
- student_emb: bfloat16 [32768, 128], P('dp'), may hold values from -64 to 64
- prototypes: float32 [32768, 128], P(('dp', 'proto')), may hold values from -0.125 to 0.125
Outputs:
- grad_prototypes: float32 [32768, 128], P(('dp', 'proto'))
- grad_student: float32 [32768, 128], P('dp')
All inputs are finite; a program needn't handle non-finite values.
Results may differ from a plain program's by a relative error of at most 0.012.
The roundings to bfloat16 on the way count: a program that leaves them out, or rounds other values in their place, can miss the bound.
Values may be sent and summed in bfloat16 or wider, within the bound.
No kernel may reach another device: no remote copies, remote signals or barrier semaphores. Data moves between devices by JAX's collectives and lax.ppermute only.
A program may use at most 64 MiB of HBM per device.

v0:
```python
import math
import jax
import jax.numpy as jnp
from jax import lax
from jax.sharding import PartitionSpec as P

ITERS = 3
teacher_temp = 0.07
student_temp = 0.1


def joined(array, axis, combine):
    everything = jax.tree.map(lambda part: lax.all_gather(part, axis), array)
    first = jax.tree.map(lambda part: part[0], everything)

    def hop(k, so_far):
        return combine(so_far, jax.tree.map(lambda part: part[k], everything))

    return lax.fori_loop(1, lax.axis_size(axis), hop, first)


def contract_rows(left, right):
    return lax.dot_general(
        left, right, (((1,), (1,)), ((), ())), preferred_element_type=jnp.float32
    )


def combine_stats(first, second):
    teacher_top = jnp.maximum(first[0], second[0])
    student_top = jnp.maximum(first[1], second[1])
    total = first[2] * jnp.exp(first[1] - student_top) + second[2] * jnp.exp(
        second[1] - student_top
    )
    return (teacher_top, student_top, total)


def per_device(teacher_emb, student_emb, prototypes):
    copies = lax.all_gather(prototypes.astype(jnp.bfloat16), "dp", axis=0, tiled=True)
    rows_here = teacher_emb.shape[0]
    width = teacher_emb.shape[1]
    block = math.gcd(rows_here, 128)
    count_blocks = rows_here // block

    def teacher_block(emb):
        logits = contract_rows(emb, copies)
        top = jnp.max(logits, axis=1)
        return (jnp.exp((logits - top[:, None]) / teacher_temp), top)

    base_local, teacher_local = lax.map(
        teacher_block, teacher_emb.reshape(count_blocks, block, width)
    )
    base_local = base_local.reshape(rows_here, -1)
    teacher_local = teacher_local.reshape(rows_here)

    def student_stats(emb):
        logits = contract_rows(emb, copies) / student_temp
        top = jnp.max(logits, axis=1)
        return (top, jnp.sum(jnp.exp(logits - top[:, None]), axis=1))

    student_local, total_local = lax.map(
        student_stats, student_emb.reshape(count_blocks, block, width)
    )
    student_local = student_local.reshape(rows_here)
    total_local = total_local.reshape(rows_here)
    teacher_top, student_top, total = joined(
        (teacher_local, student_local, total_local), "proto", combine_stats
    )
    shift = jnp.exp((teacher_local - teacher_top) / teacher_temp)
    row_scale = jnp.ones((rows_here,), jnp.float32)
    col_scale = jnp.ones((base_local.shape[1],), jnp.float32)
    for step in range(ITERS):
        partial_cols = jnp.dot(row_scale * shift, base_local, precision=lax.Precision.HIGHEST)
        col_scale = 1.0 / lax.psum(partial_cols, "dp")
        partial_rows = shift * jnp.dot(base_local, col_scale, precision=lax.Precision.HIGHEST)
        row_scale = 1.0 / lax.psum(partial_rows, "proto")
    row_factor = row_scale * shift
    student_factor = jnp.exp(student_local - student_top) / total

    def gradient_block(items):
        emb, plan, factor, local_top, soft_factor = items
        logits = contract_rows(emb, copies) / student_temp
        probs = jnp.exp(logits - local_top[:, None]) * soft_factor[:, None]
        targets = factor[:, None] * plan * col_scale[None, :]
        grads = (probs - targets).astype(jnp.bfloat16)
        return (grads, jnp.dot(grads, copies, preferred_element_type=jnp.float32) / student_temp)

    grad_logits, student_terms = lax.map(
        gradient_block,
        (
            student_emb.reshape(count_blocks, block, width),
            base_local.reshape(count_blocks, block, -1),
            row_factor.reshape(count_blocks, block),
            student_local.reshape(count_blocks, block),
            student_factor.reshape(count_blocks, block),
        ),
    )
    grad_logits = grad_logits.reshape(rows_here, -1)
    grad_student = lax.psum(student_terms.reshape(rows_here, width), "proto")
    grad_prototypes = lax.psum_scatter(
        lax.dot_general(
            grad_logits, student_emb, (((0,), (0,)), ((), ())), preferred_element_type=jnp.float32
        )
        / student_temp,
        "dp",
        scatter_dimension=0,
        tiled=True,
    )
    return (grad_prototypes, grad_student)


def solution(mesh):
    in_specs = (P("dp", None), P("dp", None), P(("dp", "proto"), None))
    out_specs = (P(("dp", "proto"), None), P("dp", None))
    return jax.shard_map(
        per_device, mesh=mesh, in_specs=in_specs, out_specs=out_specs, check_vma=False
    )
```

profile of v0, /device:TPU:2, one launch (start us, length us, event | category | flops | bytes accessed | tf_op | source)
XLA Modules:
  0.0 1962.5 jit_solution(7701246373878074425)
XLA Ops:
  7.2 1.4 convert_element_type.6
  8.7 90.5 %all-gather.5.cloned.1.call-done = bf16[8192,128]{1,0:T(8,128)(2,1)} async-done(((bf16[64,128]{1,0:T(8,128)(2,1)}), bf16[8192,128]{1,0:T(8,128)(2,1)}) %all-gather.5.cloned.1.call-update) | async-done | bytes 2097168 | tf_op jit(solution)/shard_map/all_gather | solution.py:38
  99.2 6.5 while.55
  99.2 2.4 fusion.65
  102.5 2.4 fusion.65
  105.7 7.8 all-gather.1
  113.6 10.0 while.56
  113.6 2.4 fusion.67
  116.0 2.6 bitcast_dynamic-update-slice_fusion.4
  118.5 2.4 fusion.67
  120.9 2.6 bitcast_dynamic-update-slice_fusion.4
  123.6 9.3 all-gather
  132.9 7.0 all-gather.2
  140.1 7.4 fusion.29
  147.5 490.9 %psum.49 = f32[8192]{0:T(1024)S(1)} all-reduce(f32[8192]{0:T(1024)S(1)} %bitcast.163), channel_id=1, replica_groups=mesh['dp'=128,'proto'=4] {'dp'}, use_global_device_ids=true, to_apply=%region_9.10 | all-reduce | flops 8192 | bytes 65536 | tf_op jit(solution)/shard_map/psum | solution.py:73
  638.4 8.9 fusion.30
  647.3 9.9 psum.50
  657.3 7.4 fusion.31
  664.7 490.9 %psum.51 = f32[8192]{0:T(1024)S(1)} all-reduce(f32[8192]{0:T(1024)S(1)} %bitcast.160), channel_id=1, replica_groups=mesh['dp'=128,'proto'=4] {'dp'}, use_global_device_ids=true, to_apply=%region_11.12 | all-reduce | flops 8192 | bytes 65536 | tf_op jit(solution)/shard_map/psum | solution.py:73
  1155.5 8.9 fusion.32
  1164.5 7.7 psum.52
  1172.2 7.4 fusion.33
  1179.6 491.1 %psum.53 = f32[8192]{0:T(1024)S(1)} all-reduce(f32[8192]{0:T(1024)S(1)} %bitcast.162), channel_id=1, replica_groups=mesh['dp'=128,'proto'=4] {'dp'}, use_global_device_ids=true, to_apply=%region_13.14 | all-reduce | flops 8192 | bytes 65536 | tf_op jit(solution)/shard_map/psum | solution.py:73
  1670.7 9.0 fusion.34
  1679.8 9.7 psum.54
  1689.6 11.7 while.58
  1689.6 5.1 bitcast_dynamic-update-slice_fusion.5
  1695.5 5.0 bitcast_dynamic-update-slice_fusion.5
  1702.0 5.4 convolution_multiply_fusion.3
  1707.4 38.4 %all-reduce.2.cloned.1.call-done = f32[256,128]{1,0:T(8,128)} async-done(((f32[256,128]{1,0:T(8,128)}), f32[256,128]{1,0:T(8,128)}) %all-reduce.2.cloned.1.call-update) | async-done | bytes 131088 | tf_op jit(solution)/shard_map/psum | solution.py:98
  1745.8 208.6 %reduce-scatter.2.cloned.1.call-done = f32[64,128]{1,0:T(8,128)} async-done(((f32[8192,128]{1,0:T(8,128)}), f32[64,128]{1,0:T(8,128)}) %reduce-scatter.2.cloned.1.call-update) | async-done | bytes 32784 | tf_op jit(solution)/shard_map/reduce_scatter | solution.py:99
  1954.4 1.6 copy.62
  (64 shorter events, 4.6 us)
Async XLA Ops:
  7.2 92.1 %all-gather.5.cloned.1.call-start = ((), (), s32[]{:S(2)}) async-start(), calls=%async_computation.1 | async-start | bytes 2113536 | tf_op jit(solution)/shard_map/all_gather | solution.py:38
  8.6 1737.2 %all-reduce.2.cloned.1.call-start = ((), (), s32[]{:S(2)}) async-start(), calls=%async_computation.3 | async-start | bytes 262144 | tf_op jit(solution)/shard_map/psum | solution.py:98
  99.2 14.3 copy-start.2
  1670.7 18.8 copy-start
  1670.7 18.8 copy-start.1
  1701.3 0.7 copy-start.3
  1701.9 252.5 %reduce-scatter.2.cloned.1.call-start = ((), (), s32[]{:S(2)}) async-start(), calls=%async_computation.2 | async-start | bytes 4227072 | tf_op jit(solution)/shard_map/reduce_scatter | solution.py:99
Sparse Core Ops, SparseCore 0:
  11.7 87.4 all-gather.4
  1702.1 43.7 all-reduce.1
  1751.4 202.9 reduce-scatter.1
where the time goes:
time: 1960 us
  blocking collectives  1520 us (78%)
  waiting for transfers between devices  338 us (17%)
  matrix products  75.6 us (4%)
    psum x3, blocking collectives, per_device(): col_scale = 1.0 / lax.psum(partial_cols, 'dp')  1470 us
    reduce_scatter x1, waiting for transfers between devices, per_device(): lax.psum_scatter(lax.dot_general(grad_logits, student_emb, (((0,), (0,)),...  209 us
    all_gather x1, waiting for transfers between devices, per_device(): lax.all_gather(prototypes.astype(jnp.bfloat16), 'dp', axis=0, tiled=True)  90.5 us
  transfers between devices with their start and end apart: 3, of which 3 were waited for; matrix products, arithmetic and copies ran while one was open for 0% of the time, Pallas kernels for 0%

commit v1 on v0

--- a/solution.py
+++ b/solution.py
@@ -35,7 +35,11 @@
 
 
 def per_device(teacher_emb, student_emb, prototypes):
-    copies = lax.all_gather(prototypes.astype(jnp.bfloat16), "dp", axis=0, tiled=True)
+    own = prototypes.astype(jnp.bfloat16)
+    size = lax.axis_size("dp")
+    tiles = jnp.stack([own for _ in range(size)])
+    tiles = lax.all_to_all(tiles, "dp", split_axis=0, concat_axis=0)
+    copies = jnp.concatenate(tiles, axis=0)
     rows_here = teacher_emb.shape[0]
     width = teacher_emb.shape[1]
     block = math.gcd(rows_here, 128)

time: 1960 us -> 1880 us (0.959)
  waiting for transfers between devices: 338 us -> 244 us
    all_gather x1 -> x0, waiting for transfers between devices: 90.5 us -> none  [per_device(): lax.all_gather(prototypes.astype(jnp.bfloat16), 'dp', axis=0, tiled=True)]
    all_to_all x0 -> x1, waiting for transfers between devices: none -> 52.5 us  [per_device(): tiles = lax.all_to_all(tiles, 'dp', split_axis=0, concat_axis=0)]
    reduce_scatter x1, waiting for transfers between devices: 209 us -> 156 us  [per_device(): lax.psum_scatter(lax.dot_general(grad_logits, student_emb, (((0,), (0,)),...]
where the time goes in v1:
time: 1880 us
  blocking collectives  1520 us (81%)
  waiting for transfers between devices  244 us (13%)
  matrix products  69 us (4%)
    psum x3, blocking collectives, per_device(): col_scale = 1.0 / lax.psum(partial_cols, 'dp')  1470 us
    reduce_scatter x1, waiting for transfers between devices, per_device(): lax.psum_scatter(lax.dot_general(grad_logits, student_emb, (((0,), (0,)),...  156 us
    all_to_all x1, waiting for transfers between devices, per_device(): tiles = lax.all_to_all(tiles, 'dp', split_axis=0, concat_axis=0)  52.5 us
  transfers between devices with their start and end apart: 3, of which 3 were waited for; matrix products, arithmetic and copies ran while one was open for 0% of the time, Pallas kernels for 0%

profile of v1, /device:TPU:2, one launch (start us, length us, event | category | flops | bytes accessed | tf_op | source)
XLA Modules:
  0.0 1883.4 jit_solution(12072566992711255181)
XLA Ops:
  8.0 0.8 convert_element_type.6
  8.8 1.9 stack.2
  10.7 17.8 all-to-all-start
  28.6 52.5 %all-to-all-done = bf16[128,64,128]{2,1,0:T(8,128)(2,1)S(1)} async-done(((bf16[128,64,128]{2,1,0:T(8,128)(2,1)}), bf16[128,64,128]{2,1,0:T(8,128)(2,1)S(1)}, u32[]{:S(2)}, u32[]{:S(2)}) %all-to-all-start) | async-done | bytes 2097184 | tf_op jit(solution)/shard_map/all_to_all | solution.py:41
  81.1 3.3 while.55
  81.1 0.8 fusion.65
  82.7 0.8 fusion.65
  84.3 7.8 all-gather.1
  92.2 6.8 while.56
  93.0 2.6 bitcast_dynamic-update-slice_fusion.4
  96.4 2.6 bitcast_dynamic-update-slice_fusion.4
  99.0 9.4 all-gather
  108.4 7.0 all-gather.2
  115.6 7.4 fusion.29
  123.0 491.0 %psum.49 = f32[8192]{0:T(1024)S(1)} all-reduce(f32[8192]{0:T(1024)S(1)} %bitcast.165), channel_id=1, replica_groups=mesh['dp'=128,'proto'=4] {'dp'}, use_global_device_ids=true, to_apply=%region_9.10 | all-reduce | flops 8192 | bytes 65536 | tf_op jit(solution)/shard_map/psum | solution.py:77
  614.1 8.9 fusion.30
  623.0 9.7 psum.50
  632.7 7.4 fusion.31
  640.2 490.9 %psum.51 = f32[8192]{0:T(1024)S(1)} all-reduce(f32[8192]{0:T(1024)S(1)} %bitcast.162), channel_id=1, replica_groups=mesh['dp'=128,'proto'=4] {'dp'}, use_global_device_ids=true, to_apply=%region_11.12 | all-reduce | flops 8192 | bytes 65536 | tf_op jit(solution)/shard_map/psum | solution.py:77
  1131.0 8.9 fusion.32
  1139.9 8.0 psum.52
  1147.9 7.4 fusion.33
  1155.3 490.9 %psum.53 = f32[8192]{0:T(1024)S(1)} all-reduce(f32[8192]{0:T(1024)S(1)} %bitcast.164), channel_id=1, replica_groups=mesh['dp'=128,'proto'=4] {'dp'}, use_global_device_ids=true, to_apply=%region_13.14 | all-reduce | flops 8192 | bytes 65536 | tf_op jit(solution)/shard_map/psum | solution.py:77
  1646.2 8.9 fusion.34
  1655.1 9.7 psum.54
  1664.9 11.7 while.58
  1664.9 5.1 bitcast_dynamic-update-slice_fusion.5
  1670.8 5.0 bitcast_dynamic-update-slice_fusion.5
  1677.3 5.4 convolution_multiply_fusion.3
  1682.7 35.5 %all-reduce.2.cloned.1.call-done = f32[256,128]{1,0:T(8,128)} async-done(((f32[256,128]{1,0:T(8,128)}), f32[256,128]{1,0:T(8,128)}) %all-reduce.2.cloned.1.call-update) | async-done | bytes 131088 | tf_op jit(solution)/shard_map/psum | solution.py:102
  1718.3 156.1 %reduce-scatter.2.cloned.1.call-done = f32[64,128]{1,0:T(8,128)} async-done(((f32[8192,128]{1,0:T(8,128)}), f32[64,128]{1,0:T(8,128)}) %reduce-scatter.2.cloned.1.call-update) | async-done | bytes 32784 | tf_op jit(solution)/shard_map/reduce_scatter | solution.py:103
  1874.4 1.6 copy.62
  (62 shorter events, 6.1 us)
Async XLA Ops:
  8.0 73.1 %copy-start = (bf16[256,128]{1,0:T(8,128)(2,1)S(1)}, bf16[256,128]{1,0:T(8,128)(2,1)}, u32[]{:S(2)}) copy-start(bf16[256,128]{1,0:T(8,128)(2,1)} %param.12) | copy-start | bytes 196612
  10.7 70.4 %all-to-all-start = ((bf16[128,64,128]{2,1,0:T(8,128)(2,1)}), bf16[128,64,128]{2,1,0:T(8,128)(2,1)S(1)}, u32[]{:S(2)}, u32[]{:S(2)}) async-start(bf16[128,64,128]{2,1,0:T(8,128)(2,1)} %stack.2), calls=%async_computation | async-start | bytes 4194304 | tf_op jit(solution)/shard_map/all_to_all | solution.py:41
  28.5 1689.8 %all-reduce.2.cloned.1.call-start = ((), (), s32[]{:S(2)}) async-start(), calls=%async_computation.3 | async-start | bytes 262144 | tf_op jit(solution)/shard_map/psum | solution.py:102
  81.1 11.1 copy-start.1
  1676.5 0.7 copy-start.2
  1677.2 197.1 %reduce-scatter.2.cloned.1.call-start = ((), (), s32[]{:S(2)}) async-start(), calls=%async_computation.2 | async-start | bytes 4227072 | tf_op jit(solution)/shard_map/reduce_scatter | solution.py:103
Sparse Core Ops, SparseCore 0:
  1677.3 40.8 all-reduce.1
Sparse Core Ops, SparseCore 1:
  1682.8 191.5 reduce-scatter.1
